TPU v7x, 256 devices: a whole 4x4x8 slice. The times are simulated.
256 devices in a mesh: req: 32 (over y, z_lo, core), tp: 8 (over x, z_hi).
Axes of the slice: x: 4, y: 4, z: 8 (z_hi: 2, z_lo: 4; z = z_hi * 4 + z_lo), core: 2. Of those that a mesh axis runs over, the one named last changes fastest.
Arguments:
- hidden_in: bfloat16 [8192, 2048], P('req', 'tp'), may hold values from -6 to 6
- embeds: bfloat16 [8192, 2048], P('req', 'tp'), may hold values from -6 to 6
- seg_ids: int32 [8192], replicated, may hold values from 0 to 15, never falling along the last dimension, each value on 1 to 2048 neighbouring positions
- mamba_gain: float32 [2048], replicated, may hold values from 0.5 to 1.5
- w_z: bfloat16 [2048, 2048], P(None, 'tp'), may hold values from -0.125 to 0.125
- w_x: bfloat16 [2048, 2048], P(None, 'tp'), may hold values from -0.125 to 0.125
- w_bc: bfloat16 [2048, 256], P('tp'), may hold values from -0.125 to 0.125
- w_dt: bfloat16 [2048, 32], P(None, 'tp'), may hold values from -0.125 to 0.125
- dt_bias: float32 [32], P('tp'), may hold values from -2 to 0
- decay_rate: float32 [32], P('tp'), may hold values from 0.0009765625 to 0.048828125
- conv_x: float32 [4, 2048], P(None, 'tp'), may hold values from -3 to 3
- conv_bc: float32 [4, 256], replicated, may hold values from -3 to 3
- skip_gain: float32 [32], P('tp'), may hold values from 0.5 to 1.5
- gate_gain: float32 [2048], P('tp'), may hold values from 0.5 to 1.5
- w_out: bfloat16 [2048, 2048], P('tp'), may hold values from -0.125 to 0.125
- attn_gain: float32 [4096], replicated, may hold values from 0.5 to 1.5
- w_qkv: bfloat16 [4096, 3, 2048], P(None, None, 'tp'), may hold values from -0.375 to 0.375
- adapter_down: bfloat16 [4096, 384], P('tp'), may hold values from -0.09375 to 0.09375
- adapter_up: bfloat16 [3, 128, 2048], P(None, None, 'tp'), may hold values from -0.5 to 0.5
- w_o: bfloat16 [2048, 2048], P('tp'), may hold values from -0.125 to 0.125
Outputs:
- hidden_out: bfloat16 [8192, 2048], P('req', 'tp')
- ssm_states: float32 [32, 32, 64, 128], P('req', 'tp')
- kv_cache: bfloat16 [8192, 2, 2048], P('req', None, 'tp')
Inputs may be any that keep to these rules, and one draw needn't show every extreme that they name: `seg_ids`: segment ids never fall; each of the 16 requests holds 1 to 2048 consecutive tokens and one holds exactly 2048.
All inputs are finite; a program needn't handle non-finite values.
Results may differ from a plain program's by a relative error of at most 0.013.
Values may be sent and summed in bfloat16 or wider, within the bound.
No kernel may reach another device: no remote copies, remote signals or barrier semaphores. Data moves between devices by JAX's collectives and lax.ppermute only.
A program may use at most 128 MiB of HBM per device.

v0:
```python
import math
import jax
import jax.numpy as jnp
from jax import lax
from jax.sharding import PartitionSpec as P

AHD = 128
highest = lax.Precision.HIGHEST
epsilon = 1e-05


def from_behind(block, axis, distance):
    devices = range(lax.axis_size(axis))
    route = [(i - distance, i) for i in devices if i - distance in devices]
    return lax.ppermute(block, axis, route)


def carried_in_2(value, axis, join, neutral):
    count, mine = (lax.axis_size(axis), lax.axis_index(axis))
    pieces = jax.tree.map(lambda part: lax.all_gather(part, axis), value)
    so_far = jax.tree.map(
        lambda part, zero: jnp.full_like(part, 0) + jnp.asarray(zero, part.dtype), value, neutral
    )

    def lap(position, so_far):
        longer = join(so_far, jax.tree.map(lambda part: part[position], pieces))
        return jax.tree.map(lambda new, old: jnp.where(position < mine, new, old), longer, so_far)

    return lax.fori_loop(0, count - 1, lap, so_far)


def rms_rows(values, gain):
    values = values.astype(jnp.float32)
    factor = lax.rsqrt(jnp.mean(values * values, axis=-1, keepdims=True) + epsilon)
    return values * factor * gain


def positions_of(seg_all):
    total_rows = seg_all.shape[0]
    indices = jnp.arange(total_rows, dtype=jnp.int32)
    begins = jnp.concatenate([jnp.ones((1,), dtype=bool), seg_all[1:] != seg_all[:-1]])
    first_index = lax.cummax(jnp.where(begins, indices, jnp.zeros_like(indices)), axis=0)
    return indices - first_index


def rotate(values, places):
    half_dim = values.shape[-1] // 2
    freqs = jnp.exp(-jnp.log(10000.0) * jnp.arange(half_dim, dtype=jnp.float32) / half_dim)
    angles = places.astype(jnp.float32)[:, None] * freqs[None, :]
    cosine = jnp.cos(angles)[:, None, :]
    sine = jnp.sin(angles)[:, None, :]
    first_half = values[..., :half_dim]
    second_half = values[..., half_dim:]
    return jnp.concatenate(
        [first_half * cosine - second_half * sine, second_half * cosine + first_half * sine],
        axis=-1,
    )


def conv_rows(extended, seg_extended, kernel, seg_now):
    kernel_len = kernel.shape[0]
    rows_out = seg_now.shape[0]
    result = jnp.zeros((rows_out, extended.shape[1]), jnp.float32)
    for offset in range(kernel_len):
        window_rows = extended[offset : offset + rows_out]
        matches = (seg_extended[offset : offset + rows_out] == seg_now)[:, None]
        result = result + jnp.where(matches, window_rows * kernel[offset][None, :], 0.0)
    return jax.nn.silu(result)


def ssd_block(
    inner, write_rows, read_rows, steps_dt, log_decay, seg_block, seg_before, state_prev, skip_gain
):
    length = inner.shape[0]
    cumul = jnp.cumsum(log_decay, axis=0)
    order = jnp.arange(length, dtype=jnp.int32)
    within = (seg_block[:, None] == seg_block[None, :]) & (order[:, None] >= order[None, :])
    spread = cumul.T[:, :, None] - cumul.T[:, None, :]
    decays = jnp.where(within[None], jnp.exp(jnp.minimum(spread, 0.0)), 0.0)
    intersection = jnp.dot(read_rows, write_rows.T, precision=highest)
    mixing = decays * intersection[None] * steps_dt.T[:, None, :]
    local_out = jnp.einsum("hts,shp->thp", mixing, inner, precision=highest)
    carried = jnp.where((seg_block == seg_before)[:, None], jnp.exp(cumul), 0.0)
    from_state = jnp.einsum("tn,hpn->thp", read_rows, state_prev, precision=highest)
    outputs = local_out + carried[:, :, None] * from_state + skip_gain[None, :, None] * inner
    tail_weight = (
        jnp.where((seg_block == seg_block[-1])[:, None], jnp.exp(cumul[-1][None, :] - cumul), 0.0)
        * steps_dt
    )
    keep_factor = jnp.where(seg_block[-1] == seg_before, jnp.exp(cumul[-1]), 0.0)
    state_next = keep_factor[:, None, None] * state_prev + jnp.einsum(
        "sh,shp,sn->hpn", tail_weight, inner, write_rows, precision=highest
    )
    return (outputs, state_next)


def accumulate_rows(left_rows, weight_rows):
    return jnp.dot(left_rows, weight_rows, preferred_element_type=jnp.float32)


def combine_states(earlier, later):
    return (earlier[0] * later[0], later[0][:, None, None] * earlier[1] + later[1])


def on_device(
    hidden_in,
    embeds,
    seg_ids,
    mamba_gain,
    w_z,
    w_x,
    w_bc,
    w_dt,
    dt_bias,
    decay_rate,
    conv_x,
    conv_bc,
    skip_gain,
    gate_gain,
    w_out,
    attn_gain,
    w_qkv,
    adapter_down,
    adapter_up,
    w_o,
):
    rows_here = hidden_in.shape[0]
    tensor_size = lax.axis_size("tp")
    req_rank = lax.axis_index("req")
    first_row = req_rank * rows_here
    full_hidden, full_embeds = (
        lax.all_gather(hidden_in, "tp", axis=1, tiled=True),
        lax.all_gather(embeds, "tp", axis=1, tiled=True),
    )
    normed = rms_rows(full_hidden, mamba_gain).astype(jnp.bfloat16)
    gate_z = jnp.dot(normed, w_z, preferred_element_type=jnp.float32)
    inner_x = jnp.dot(normed, w_x, preferred_element_type=jnp.float32)
    raw_dt = jnp.dot(normed, w_dt, preferred_element_type=jnp.float32)
    state_io = accumulate_rows(normed, lax.all_gather(w_bc, "tp", axis=0, tiled=True))
    mixed_in = jnp.concatenate([inner_x, state_io], axis=1)
    kernel_len = conv_x.shape[0]
    tail_rows = mixed_in[rows_here - (kernel_len - 1) :]
    prior_rows = from_behind(tail_rows, "req", 1)
    extended = jnp.concatenate([prior_rows, mixed_in], axis=0)
    seg_padded = jnp.concatenate(
        [jnp.full((kernel_len - 1,), -1, dtype=jnp.int32), seg_ids], axis=0
    )
    seg_extended = lax.dynamic_slice_in_dim(seg_padded, first_row, rows_here + kernel_len - 1, 0)
    seg_now = lax.dynamic_slice_in_dim(seg_ids, first_row, rows_here, 0)
    kernel = jnp.concatenate([conv_x, conv_bc], axis=1)
    conv_out = conv_rows(extended, seg_extended, kernel, seg_now)
    inner_here = w_z.shape[1]
    heads_here = w_dt.shape[1]
    head_dim = inner_here // heads_here
    state_dim = state_io.shape[1] // 2
    inner_c = conv_out[:, :inner_here].reshape(rows_here, heads_here, head_dim)
    write_rows = conv_out[:, inner_here : inner_here + state_dim]
    read_rows = conv_out[:, inner_here + state_dim :]
    steps_dt = jax.nn.softplus(raw_dt + dt_bias)
    log_decay = -steps_dt * decay_rate
    seg_before = jnp.where(req_rank > 0, seg_ids[jnp.maximum(first_row - 1, 0)], -1)
    seg_prior = jnp.concatenate([seg_before[None], seg_now[:-1]], axis=0)
    block_rows = math.gcd(rows_here, 256)
    count_blocks = rows_here // block_rows
    block_before = seg_prior.reshape(count_blocks, block_rows)[:, 0]

    def ssd_step(state_prev, pieces):
        blk_inner, blk_write, blk_read, blk_dt, blk_decay, blk_seg, blk_before = pieces
        outputs, state_next = ssd_block(
            blk_inner,
            blk_write,
            blk_read,
            blk_dt,
            blk_decay,
            blk_seg,
            blk_before,
            state_prev,
            skip_gain,
        )
        return (state_next, outputs)

    zero_state = jnp.zeros((heads_here, head_dim, state_dim), jnp.float32)
    local_state, local_out = lax.scan(
        ssd_step,
        zero_state,
        (
            inner_c.reshape(count_blocks, block_rows, heads_here, head_dim),
            write_rows.reshape(count_blocks, block_rows, state_dim),
            read_rows.reshape(count_blocks, block_rows, state_dim),
            steps_dt.reshape(count_blocks, block_rows, heads_here),
            log_decay.reshape(count_blocks, block_rows, heads_here),
            seg_now.reshape(count_blocks, block_rows),
            block_before,
        ),
    )
    local_out = local_out.reshape(rows_here, heads_here, head_dim)
    cumul_all = jnp.cumsum(log_decay, axis=0)
    through = jnp.where(seg_now[-1] == seg_before, jnp.exp(cumul_all[-1]), 0.0)
    incoming = carried_in_2(
        (through, local_state),
        "req",
        combine_states,
        (jnp.ones_like(through), jnp.zeros_like(local_state)),
    )
    carried_in = incoming[1]
    carried = jnp.where((seg_now == seg_before)[:, None], jnp.exp(cumul_all), 0.0)
    from_state = jnp.einsum("tn,hpn->thp", read_rows, carried_in, precision=highest)
    ssm_y = local_out + carried[:, :, None] * from_state
    final_state = local_state + through[:, None, None] * carried_in
    gated_rows = ssm_y.reshape(rows_here, inner_here) * jax.nn.silu(gate_z)
    square_sum = lax.psum(jnp.sum(gated_rows * gated_rows, axis=1), "tp")
    factor = lax.rsqrt(square_sum / (inner_here * tensor_size) + epsilon)
    gated_norm = (gated_rows * factor[:, None] * gate_gain).astype(jnp.bfloat16)
    mix_terms = jnp.dot(gated_norm, w_out, preferred_element_type=jnp.float32)
    mix_share = lax.psum_scatter(mix_terms, "tp", scatter_dimension=1, tiled=True)
    mid_here = (hidden_in.astype(jnp.float32) + mix_share).astype(jnp.bfloat16)
    mid_full = lax.all_gather(mid_here, "tp", axis=1, tiled=True)
    joined = jnp.concatenate([mid_full, full_embeds], axis=1)
    attn_in = rms_rows(joined, attn_gain).astype(jnp.bfloat16)
    low_sum = accumulate_rows(attn_in, lax.all_gather(adapter_down, "tp", axis=0, tiled=True))
    low_rank = low_sum.astype(jnp.bfloat16)
    rank_cols = adapter_up.shape[1]
    cols_here = w_qkv.shape[2]
    heads_attn = cols_here // AHD
    projected = jnp.dot(
        attn_in, w_qkv.reshape(w_qkv.shape[0], 3 * cols_here), preferred_element_type=jnp.float32
    ).reshape(rows_here, 3, cols_here)
    projected = projected + jnp.einsum(
        "tjr,jrc->tjc",
        low_rank.reshape(rows_here, 3, rank_cols),
        adapter_up,
        preferred_element_type=jnp.float32,
    )
    places = lax.dynamic_slice_in_dim(positions_of(seg_ids), first_row, rows_here, 0)
    queries = rotate(projected[:, 0].reshape(rows_here, heads_attn, AHD), places).astype(
        jnp.bfloat16
    )
    key_rows = rotate(projected[:, 1].reshape(rows_here, heads_attn, AHD), places).astype(
        jnp.bfloat16
    )
    value_rows = projected[:, 2].astype(jnp.bfloat16)
    kv_pair = jnp.stack([key_rows.reshape(rows_here, cols_here), value_rows], axis=1)
    query_index = first_row + jnp.arange(rows_here, dtype=jnp.int32)
    inv_root = 1.0 / math.sqrt(AHD)

    def absorb(running, block_kv, first_key):
        row_top, denom_sum, weighted = running
        key_count = block_kv.shape[0]
        key_index = first_key + jnp.arange(key_count, dtype=jnp.int32)
        key_seg = lax.dynamic_slice_in_dim(seg_ids, jnp.maximum(first_key, 0), key_count, 0)
        allowed = (
            (key_seg[None, :] == seg_now[:, None])
            & (key_index[None, :] <= query_index[:, None])
            & (key_index[None, :] >= 0)
        )
        block_keys = block_kv[:, 0].reshape(key_count, heads_attn, AHD)
        block_vals = block_kv[:, 1].reshape(key_count, heads_attn, AHD)
        scores = (
            jnp.einsum("qhe,khe->hqk", queries, block_keys, preferred_element_type=jnp.float32)
            * inv_root
        )
        masked = jnp.where(allowed[None], scores, -1e30)
        new_top = jnp.maximum(row_top, jnp.max(masked, axis=-1))
        weights = jnp.where(allowed[None], jnp.exp(scores - new_top[:, :, None]), 0.0)
        shrink = jnp.exp(row_top - new_top)
        denom_sum = denom_sum * shrink + jnp.sum(weights, axis=-1)
        weighted = weighted * shrink[:, :, None] + jnp.einsum(
            "hqk,khe->hqe",
            weights.astype(jnp.bfloat16),
            block_vals,
            preferred_element_type=jnp.float32,
        )
        return (new_top, denom_sum, weighted)

    start_state = (
        jnp.full((heads_attn, rows_here), -1e30, jnp.float32),
        jnp.zeros((heads_attn, rows_here), jnp.float32),
        jnp.zeros((heads_attn, rows_here, AHD), jnp.float32),
    )
    reach_hops = lax.axis_size("req") // 4
    running = absorb(start_state, kv_pair, first_row)
    moving = kv_pair
    for hop_count in range(1, reach_hops + 1):
        moving = from_behind(moving, "req", 1)
        running = absorb(running, moving, first_row - hop_count * rows_here)
    row_top, denom_sum, weighted = running
    attended = (weighted / denom_sum[:, :, None]).astype(jnp.bfloat16)
    attended = attended.transpose(1, 0, 2).reshape(rows_here, cols_here)
    attn_terms = jnp.dot(attended, w_o, preferred_element_type=jnp.float32)
    attn_share = lax.psum_scatter(
        attn_terms.astype(jnp.bfloat16), "tp", scatter_dimension=1, tiled=True
    ).astype(jnp.float32)
    hidden_out = (mid_here.astype(jnp.float32) + attn_share).astype(jnp.bfloat16)
    return (hidden_out, final_state[None], kv_pair)


def solution(mesh):
    in_specs = (
        P("req", "tp"),
        P("req", "tp"),
        P(),
        P(),
        P(None, "tp"),
        P(None, "tp"),
        P("tp", None),
        P(None, "tp"),
        P("tp"),
        P("tp"),
        P(None, "tp"),
        P(),
        P("tp"),
        P("tp"),
        P("tp", None),
        P(),
        P(None, None, "tp"),
        P("tp", None),
        P(None, None, "tp"),
        P("tp", None),
    )
    out_specs = (P("req", "tp"), P("req", "tp", None, None), P("req", None, "tp"))
    return jax.shard_map(
        on_device, mesh=mesh, in_specs=in_specs, out_specs=out_specs, check_vma=False
    )
```

profile of v0, /device:TPU:8, one launch (start us, length us, event | category | flops | bytes accessed | tf_op | source)
XLA Modules:
  0.0 785.6 jit_solution(5551168740319205681)
XLA Ops:
  18.1 56.8 %all-gather.9.cloned.1.call-done = bf16[256,2048]{1,0:T(8,128)(2,1)} async-done(((bf16[256,256]{1,0:T(8,128)(2,1)}), bf16[256,2048]{1,0:T(8,128)(2,1)}) %all-gather.9.cloned.1.call-update) | async-done | bytes 1048592 | tf_op jit(solution)/shard_map/all_gather | solution.py:132
  76.5 58.3 %all-gather.11.cloned.1.call-done = bf16[2048,256]{1,0:T(8,128)(2,1)} async-done(((bf16[256,256]{1,0:T(8,128)(2,1)}), bf16[2048,256]{1,0:T(8,128)(2,1)}) %all-gather.11.cloned.1.call-update) | async-done | bytes 1048592 | tf_op jit(solution)/shard_map/all_gather | solution.py:139
  134.8 2.2 fusion.161
  139.1 1.9 collective-permute-start
  145.2 4.3 collective-permute-done
  153.5 1.9 and_and_fusion.6
  156.2 34.6 %all-gather.1 = f32[32,1,4]{2,1,0:T(1,128)} all-gather(f32[1,1,4]{2,1,0:T(1,128)} %bitcast.388), channel_id=1, replica_groups=mesh['req'=32,'tp'=8] {'req'}, dimensions={0}, use_global_device_ids=true | all-gather | bytes 528 | tf_op jit(solution)/shard_map/all_gather | solution.py:20
  191.2 2.2 convolution_bitcast_fusion.10
  194.4 15.0 %all-gather.19.cloned.1.call-done = f32[128,64,128]{2,1,0:T(8,128)} async-done(((f32[4,64,128]{2,1,0:T(8,128)}), f32[128,64,128]{2,1,0:T(8,128)}) %all-gather.19.cloned.1.call-update) | async-done | bytes 4194320 | tf_op jit(solution)/shard_map/all_gather | solution.py:20
  209.4 52.5 %while.9 = (s32[]{:T(128)}, f32[4,64,128]{2,1,0:T(8,128)S(1)}, s32[]{:T(128)}, f32[32,4]{1,0:T(8,128)}, f32[32,4,64,128]{3,2,1,0:T(8,128)}, /*index=5*/s32[]{:T(128)}, s32[]{:T(128)}) while((s32[]{:T(128)}, f32[4,64,128]{2,1,0:T(8,128)S(1)}, s32[]{:T(128)}, f32[32,4]{1,0:T(8,128)}, f32[32,4,64,128]{3,2,1,0:T(8,128)}, ...), condition=%wide.region_4.5_spmd.clone, body=%wide.region_3.4_spmd.clone.sunk | while | flops 131076 | bytes 393369 | solution.py:29
  262.3 1.9 multiply_reduce_fusion
  264.2 29.9 %psum.7 = f32[256]{0:T(256)S(1)} all-reduce(f32[256]{0:T(256)S(1)} %get-tuple-element.279), channel_id=1, replica_groups=mesh['req'=32,'tp'=8] {'tp'}, use_global_device_ids=true, to_apply=%region_6.7 | all-reduce | flops 256 | bytes 2048 | tf_op jit(solution)/shard_map/psum | solution.py:211
  296.7 89.3 %reduce-scatter.3.cloned.1.call-done = f32[256,256]{1,0:T(8,128)} async-done(((f32[256,2048]{1,0:T(8,128)}), f32[256,256]{1,0:T(8,128)}) %reduce-scatter.3.cloned.1.call-update) | async-done | bytes 262160 | tf_op jit(solution)/shard_map/reduce_scatter | solution.py:215
  388.6 8.8 %copy.99 = bf16[4096,3,256]{0,2,1:T(8,128)(2,1)} copy(bf16[4096,3,256]{2,0,1:T(8,128)(2,1)} %param.38) | data formatting | bytes 12582912 | tf_op args[16]
  399.5 46.1 %all-gather.15.cloned.1.call-done = bf16[256,2048]{1,0:T(8,128)(2,1)} async-done(((bf16[256,256]{1,0:T(8,128)(2,1)}), bf16[256,2048]{1,0:T(8,128)(2,1)}) %all-gather.15.cloned.1.call-update) | async-done | bytes 1048592 | tf_op jit(solution)/shard_map/all_gather | solution.py:133
  445.6 60.0 %all-gather.13.cloned.1.call-done = bf16[256,2048]{1,0:T(8,128)(2,1)} async-done(((bf16[256,256]{1,0:T(8,128)(2,1)}), bf16[256,2048]{1,0:T(8,128)(2,1)}) %all-gather.13.cloned.1.call-update) | async-done | bytes 1048592 | tf_op jit(solution)/shard_map/all_gather | solution.py:217
  505.6 2.0 fusion.3
  507.7 87.6 %all-gather.17.cloned.1.call-done = bf16[4096,384]{1,0:T(8,128)(2,1)} async-done(((bf16[512,384]{1,0:T(8,128)(2,1)}), bf16[4096,384]{1,0:T(8,128)(2,1)}) %all-gather.17.cloned.1.call-update) | async-done | bytes 3145744 | tf_op jit(solution)/shard_map/all_gather | solution.py:220
  595.3 3.5 convolution_convert_fusion.1
  599.0 5.1 fusion.1
  605.1 1.9 collective-permute-start.1
  607.8 7.8 collective-permute-done.1
  618.8 7.4 collective-permute-done.2
  628.4 8.1 %collective-permute-done.3 = bf16[256,2,256]{0,2,1:T(8,128)(2,1)S(1)} collective-permute-done((bf16[256,2,256]{0,2,1:T(8,128)(2,1)S(1)}, bf16[256,2,256]{0,2,1:T(8,128)(2,1)S(1)}, u32[]{:S(2)}, u32[]{:S(2)}) %collective-permute-start.3) | collective-permute-done | bytes 262176 | tf_op jit(solution)/shard_map/ppermute | solution.py:15
  636.6 1.9 collective-permute-start.4
  638.8 8.1 %collective-permute-done.4 = bf16[256,2,256]{0,2,1:T(8,128)(2,1)S(1)} collective-permute-done((bf16[256,2,256]{0,2,1:T(8,128)(2,1)S(1)}, bf16[256,2,256]{0,2,1:T(8,128)(2,1)S(1)}, u32[]{:S(2)}, u32[]{:S(2)}) %collective-permute-start.4) | collective-permute-done | bytes 262176 | tf_op jit(solution)/shard_map/ppermute | solution.py:15
  647.0 1.9 collective-permute-start.5
  649.2 8.1 %collective-permute-done.5 = bf16[256,2,256]{0,2,1:T(8,128)(2,1)S(1)} collective-permute-done((bf16[256,2,256]{0,2,1:T(8,128)(2,1)S(1)}, bf16[256,2,256]{0,2,1:T(8,128)(2,1)S(1)}, u32[]{:S(2)}, u32[]{:S(2)}) %collective-permute-start.5) | collective-permute-done | bytes 262176 | tf_op jit(solution)/shard_map/ppermute | solution.py:15
  659.6 8.1 %collective-permute-done.6 = bf16[256,2,256]{0,2,1:T(8,128)(2,1)S(1)} collective-permute-done((bf16[256,2,256]{0,2,1:T(8,128)(2,1)S(1)}, bf16[256,2,256]{0,2,1:T(8,128)(2,1)S(1)}, u32[]{:S(2)}, u32[]{:S(2)}) %collective-permute-start.6) | collective-permute-done | bytes 262176 | tf_op jit(solution)/shard_map/ppermute | solution.py:15
  670.0 8.1 %collective-permute-done.7 = bf16[256,2,256]{0,2,1:T(8,128)(2,1)S(1)} collective-permute-done((bf16[256,2,256]{0,2,1:T(8,128)(2,1)S(1)}, bf16[256,2,256]{0,2,1:T(8,128)(2,1)S(1)}, u32[]{:S(2)}, u32[]{:S(2)}) %collective-permute-start.7) | collective-permute-done | bytes 262176 | tf_op jit(solution)/shard_map/ppermute | solution.py:15
  680.3 8.1 %collective-permute-done.8 = bf16[256,2,256]{0,2,1:T(8,128)(2,1)S(1)} collective-permute-done((bf16[256,2,256]{0,2,1:T(8,128)(2,1)S(1)}, bf16[256,2,256]{0,2,1:T(8,128)(2,1)S(1)}, u32[]{:S(2)}, u32[]{:S(2)}) %collective-permute-start.8) | collective-permute-done | bytes 262176 | tf_op jit(solution)/shard_map/ppermute | solution.py:15
  695.7 81.5 %reduce-scatter.5.cloned.1.call-done = bf16[256,256]{1,0:T(8,128)(2,1)} async-done(((bf16[256,2048]{1,0:T(8,128)(2,1)}), bf16[256,256]{1,0:T(8,128)(2,1)}) %reduce-scatter.5.cloned.1.call-update) | async-done | bytes 131088 | tf_op jit(solution)/shard_map/reduce_scatter | solution.py:290
  (253 shorter events, 104.6 us)
Async XLA Ops:
  7.2 287.0 %copy-start = (bf16[256,2048]{1,0:T(8,128)(2,1)S(1)}, bf16[256,2048]{1,0:T(8,128)(2,1)}, u32[]{:S(2)}) copy-start(bf16[256,2048]{1,0:T(8,128)(2,1)} %param.36) | copy-start | bytes 3145732
  7.2 67.7 %all-gather.9.cloned.1.call-start = ((), (), s32[]{:S(2)}) async-start(), calls=%async_computation.2 | async-start | bytes 1179648 | tf_op jit(solution)/shard_map/all_gather | solution.py:132
  7.9 129.1 %copy-start.20 = (f32[2048]{0:T(1024)S(1)}, f32[2048]{0:T(1024)}, u32[]{:S(2)}) copy-start(f32[2048]{0:T(1024)} %param.25) | copy-start | bytes 24580
  7.9 126.9 %all-gather.11.cloned.1.call-start = ((), (), s32[]{:S(2)}) async-start(), calls=%async_computation.3 | async-start | bytes 1179648 | tf_op jit(solution)/shard_map/all_gather | solution.py:139
  8.7 200.7 %all-gather.19.cloned.1.call-start = ((), (), s32[]{:S(2)}) async-start(), calls=%async_computation.9 | async-start | bytes 4325376 | tf_op jit(solution)/shard_map/all_gather | solution.py:20
  74.9 62.2 %copy-start.3 = (bf16[256,2048]{1,0:T(8,128)(2,1)S(1)}, bf16[256,2048]{1,0:T(8,128)(2,1)}, u32[]{:S(2)}) copy-start(bf16[256,2048]{1,0:T(8,128)(2,1)} %all-gather.9.cloned.1.call-done) | copy-start | bytes 3145732
  76.5 64.6 %copy-start.17 = (f32[256]{0:T(256)}, f32[256]{0:T(256)S(1)}, u32[]{:S(2)}) copy-start(f32[256]{0:T(256)S(1)} %add_rsqrt_fusion.2) | copy-start | bytes 3076
  139.1 10.4 %collective-permute-start = (f32[3,512]{0,1:T(8,128)S(1)}, f32[3,512]{0,1:T(8,128)S(1)}, u32[]{:S(2)}, u32[]{:S(2)}) collective-permute-start(f32[3,512]{0,1:T(8,128)S(1)} %fusion.80), channel_id=1, source_target_pairs={{0,8},{8,16},{16,24},{24,32},{32,40},{40,48},{48,56},{56,64},{64,7... | collective-permute-start | bytes 18440 | tf_op jit(solution)/shard_map/ppermute | solution.py:15
  151.5 234.4 %reduce-scatter.3.cloned.1.call-start = ((), (), s32[]{:S(2)}) async-start(), calls=%async_computation.4 | async-start | bytes 2359296 | tf_op jit(solution)/shard_map/reduce_scatter | solution.py:215
  262.3 31.9 %copy-start.16 = (f32[256]{0:T(256)S(1)}, f32[256]{0:T(256)}, u32[]{:S(2)}) copy-start(f32[256]{0:T(256)} %param.35) | copy-start | bytes 3076
  294.1 91.8 %copy-start.8 = (bf16[256,256]{1,0:T(8,128)(2,1)S(1)}, bf16[256,256]{1,0:T(8,128)(2,1)}, u32[]{:S(2)}) copy-start(bf16[256,256]{1,0:T(8,128)(2,1)} %param.22) | copy-start | bytes 393220
  296.1 149.5 %all-gather.15.cloned.1.call-start = ((), (), s32[]{:S(2)}) async-start(), calls=%async_computation.6 | async-start | bytes 1179648 | tf_op jit(solution)/shard_map/all_gather | solution.py:133
  296.6 209.0 %all-gather.13.cloned.1.call-start = ((), (), s32[]{:S(2)}) async-start(), calls=%async_computation.5 | async-start | bytes 1179648 | tf_op jit(solution)/shard_map/all_gather | solution.py:217
  387.6 207.7 %all-gather.17.cloned.1.call-start = ((), (), s32[]{:S(2)}) async-start(), calls=%async_computation.7 | async-start | bytes 3538944 | tf_op jit(solution)/shard_map/all_gather | solution.py:220
  388.4 9.1 %copy-start.9 = (s32[8192]{0:T(1024)S(1)}, s32[8192]{0:T(1024)}, u32[]{:S(2)}) copy-start(s32[8192]{0:T(1024)} %param.24) | copy-start | bytes 98308
  388.4 10.1 %copy-start.12 = (s32[256]{0:T(256)S(1)}, s32[256]{0:T(256)}, u32[]{:S(2)}) copy-start(s32[256]{0:T(256)} %get-tuple-element.235) | copy-start | bytes 3076
  388.4 10.1 %copy-start.13 = (s32[256]{0:T(256)S(1)}, s32[256]{0:T(256)}, u32[]{:S(2)}) copy-start(s32[256]{0:T(256)} %get-tuple-element.238) | copy-start | bytes 3076
  388.4 10.1 %copy-start.14 = (s32[256]{0:T(256)S(1)}, s32[256]{0:T(256)}, u32[]{:S(2)}) copy-start(s32[256]{0:T(256)} %get-tuple-element.239) | copy-start | bytes 3076
  388.4 388.8 %reduce-scatter.5.cloned.1.call-start = ((), (), s32[]{:S(2)}) async-start(), calls=%async_computation.8 | async-start | bytes 1179648 | tf_op jit(solution)/shard_map/reduce_scatter | solution.py:290
  397.4 197.9 %copy-start.19 = (f32[4096]{0:T(1024)S(1)}, f32[4096]{0:T(1024)}, u32[]{:S(2)}) copy-start(f32[4096]{0:T(1024)} %param.37) | copy-start | bytes 49156
  445.6 149.7 %copy-start.5 = (bf16[256,2048]{1,0:T(8,128)(2,1)S(1)}, bf16[256,2048]{1,0:T(8,128)(2,1)}, u32[]{:S(2)}) copy-start(bf16[256,2048]{1,0:T(8,128)(2,1)} %all-gather.15.cloned.1.call-done) | copy-start | bytes 3145732
  599.0 5.1 copy-start.10
  605.1 10.5 %collective-permute-start.1 = (bf16[256,2,256]{0,2,1:T(8,128)(2,1)S(1)}, bf16[256,2,256]{0,2,1:T(8,128)(2,1)}, u32[]{:S(2)}, u32[]{:S(2)}) collective-permute-start(bf16[256,2,256]{0,2,1:T(8,128)(2,1)S(1)} %pad_maximum_fusion.2), channel_id=1, source_target_pairs={{0,8},{8,16},{16,24},{24,32},{32,40},{40,48},{48,56},{56,64},{64,7... | collective-permute-start | bytes 786440 | tf_op jit(solution)/shard_map/ppermute | solution.py:15
  607.3 20.8 %copy-start.6 = (pred[256,256]{0,1:T(8,128)(4,1)S(1)}, pred[256,256]{0,1:T(8,128)(4,1)}, u32[]{:S(2)}) copy-start(pred[256,256]{0,1:T(8,128)(4,1)} %get-tuple-element.258) | copy-start | bytes 196612
  615.6 10.6 %collective-permute-start.2 = (bf16[256,2,256]{0,2,1:T(8,128)(2,1)}, bf16[256,2,256]{0,2,1:T(8,128)(2,1)S(1)}, u32[]{:S(2)}, u32[]{:S(2)}) collective-permute-start(bf16[256,2,256]{0,2,1:T(8,128)(2,1)} %collective-permute-done.1), channel_id=1, source_target_pairs={{0,8},{8,16},{16,24},{24,32},{32,40},{40,48},{48,56},{56,64},{64,7... | collective-permute-start | bytes 786440 | tf_op jit(solution)/shard_map/ppermute | solution.py:15
  626.2 10.4 %collective-permute-start.3 = (bf16[256,2,256]{0,2,1:T(8,128)(2,1)S(1)}, bf16[256,2,256]{0,2,1:T(8,128)(2,1)S(1)}, u32[]{:S(2)}, u32[]{:S(2)}) collective-permute-start(bf16[256,2,256]{0,2,1:T(8,128)(2,1)S(1)} %collective-permute-done.2), channel_id=1, source_target_pairs={{0,8},{8,16},{16,24},{24,32},{32,40},{40,48},{48,56},{56,64},{64,7... | collective-permute-start | bytes 786440 | tf_op jit(solution)/shard_map/ppermute | solution.py:15
  636.6 10.4 %collective-permute-start.4 = (bf16[256,2,256]{0,2,1:T(8,128)(2,1)S(1)}, bf16[256,2,256]{0,2,1:T(8,128)(2,1)S(1)}, u32[]{:S(2)}, u32[]{:S(2)}) collective-permute-start(bf16[256,2,256]{0,2,1:T(8,128)(2,1)S(1)} %collective-permute-done.3), channel_id=1, source_target_pairs={{0,8},{8,16},{16,24},{24,32},{32,40},{40,48},{48,56},{56,64},{64,7... | collective-permute-start | bytes 786440 | tf_op jit(solution)/shard_map/ppermute | solution.py:15
  647.0 10.4 %collective-permute-start.5 = (bf16[256,2,256]{0,2,1:T(8,128)(2,1)S(1)}, bf16[256,2,256]{0,2,1:T(8,128)(2,1)S(1)}, u32[]{:S(2)}, u32[]{:S(2)}) collective-permute-start(bf16[256,2,256]{0,2,1:T(8,128)(2,1)S(1)} %collective-permute-done.4), channel_id=1, source_target_pairs={{0,8},{8,16},{16,24},{24,32},{32,40},{40,48},{48,56},{56,64},{64,7... | collective-permute-start | bytes 786440 | tf_op jit(solution)/shard_map/ppermute | solution.py:15
  657.3 10.4 %collective-permute-start.6 = (bf16[256,2,256]{0,2,1:T(8,128)(2,1)S(1)}, bf16[256,2,256]{0,2,1:T(8,128)(2,1)S(1)}, u32[]{:S(2)}, u32[]{:S(2)}) collective-permute-start(bf16[256,2,256]{0,2,1:T(8,128)(2,1)S(1)} %collective-permute-done.5), channel_id=1, source_target_pairs={{0,8},{8,16},{16,24},{24,32},{32,40},{40,48},{48,56},{56,64},{64,7... | collective-permute-start | bytes 786440 | tf_op jit(solution)/shard_map/ppermute | solution.py:15
  667.7 10.4 %collective-permute-start.7 = (bf16[256,2,256]{0,2,1:T(8,128)(2,1)S(1)}, bf16[256,2,256]{0,2,1:T(8,128)(2,1)S(1)}, u32[]{:S(2)}, u32[]{:S(2)}) collective-permute-start(bf16[256,2,256]{0,2,1:T(8,128)(2,1)S(1)} %collective-permute-done.6), channel_id=1, source_target_pairs={{0,8},{8,16},{16,24},{24,32},{32,40},{40,48},{48,56},{56,64},{64,7... | collective-permute-start | bytes 786440 | tf_op jit(solution)/shard_map/ppermute | solution.py:15
  678.1 10.4 %collective-permute-start.8 = (bf16[256,2,256]{0,2,1:T(8,128)(2,1)S(1)}, bf16[256,2,256]{0,2,1:T(8,128)(2,1)S(1)}, u32[]{:S(2)}, u32[]{:S(2)}) collective-permute-start(bf16[256,2,256]{0,2,1:T(8,128)(2,1)S(1)} %collective-permute-done.7), channel_id=1, source_target_pairs={{0,8},{8,16},{16,24},{24,32},{32,40},{40,48},{48,56},{56,64},{64,7... | collective-permute-start | bytes 786440 | tf_op jit(solution)/shard_map/ppermute | solution.py:15
  692.6 84.5 %copy-start.2 = (bf16[256,256]{1,0:T(8,128)(2,1)S(1)}, bf16[256,256]{1,0:T(8,128)(2,1)}, u32[]{:S(2)}) copy-start(bf16[256,256]{1,0:T(8,128)(2,1)} %add_convert_fusion.2) | copy-start | bytes 393220
  (8 other events, 21.0 us)
Sparse Core Ops, SparseCore 0:
  10.5 64.3 all-gather.8
  77.5 57.2 all-gather.10
  151.6 57.7 all-gather.18
  296.2 89.7 reduce-scatter.2
  388.3 57.2 all-gather.14
  448.5 57.0 all-gather.12
  508.2 87.0 all-gather.16
  694.2 82.9 reduce-scatter.4
where the time goes:
time: 788 us; the launch traced here: 786 us
  waiting for transfers between devices  566 us (72%)
  blocking collectives  64.5 us (8%)
  other arithmetic  49.5 us (6%)
  local copies, waits for them, and re-layouts  41 us (5%)
  matrix products  29.1 us (4%)
  starting transfers between devices  17.7 us (2%)
  between operations  17.7 us (2%)
    reduce_scatter x1, waiting for transfers between devices, on_device(): lax.psum_scatter(mix_terms, 'tp', scatter_dimension=1, tiled=True)  89.3 us
    all_gather x1, waiting for transfers between devices, on_device(): lax.all_gather(adapter_down, 'tp', axis=0, tiled=True)  87.6 us
    reduce_scatter x1, waiting for transfers between devices, on_device(): lax.psum_scatter(attn_terms.astype(jnp.bfloat16), 'tp', scatter_dimension...  81.5 us
    ppermute x9, waiting for transfers between devices, from_behind(): return lax.ppermute(block, axis, route)  68.4 us
    all_gather x1, waiting for transfers between devices, on_device(): mid_full = lax.all_gather(mid_here, 'tp', axis=1, tiled=True)  60 us
    all_gather x1, waiting for transfers between devices, on_device(): lax.all_gather(w_bc, 'tp', axis=0, tiled=True)  58.3 us
    all_gather x1, waiting for transfers between devices, on_device(): lax.all_gather(hidden_in, 'tp', axis=1, tiled=True)  56.8 us
    all_gather x1, waiting for transfers between devices, on_device(): lax.all_gather(embeds, 'tp', axis=1, tiled=True)  46.1 us
  transfers between devices with their start and end apart: 17, of which 17 were waited for; matrix products, arithmetic and copies ran while one was open for 5% of the time, Pallas kernels for 0%

commit v1 on v0

--- a/solution.py
+++ b/solution.py
@@ -214,7 +214,9 @@
     mix_terms = jnp.dot(gated_norm, w_out, preferred_element_type=jnp.float32)
     mix_share = lax.psum_scatter(mix_terms, "tp", scatter_dimension=1, tiled=True)
     mid_here = (hidden_in.astype(jnp.float32) + mix_share).astype(jnp.bfloat16)
-    mid_full = lax.all_gather(mid_here, "tp", axis=1, tiled=True)
+    mid_full = jnp.concatenate(
+        lax.all_to_all(jnp.stack([mid_here] * lax.axis_size("tp")), "tp", 0, 0), axis=1
+    )
     joined = jnp.concatenate([mid_full, full_embeds], axis=1)
     attn_in = rms_rows(joined, attn_gain).astype(jnp.bfloat16)
     low_sum = accumulate_rows(attn_in, lax.all_gather(adapter_down, "tp", axis=0, tiled=True))

time: 788 us -> 719 us (0.912)
  waiting for transfers between devices: 566 us -> 516 us
  local copies, waits for them, and re-layouts: 41 us -> 21 us
    all_gather x1 -> x0, waiting for transfers between devices: 60 us -> none  [on_device(): mid_full = lax.all_gather(mid_here, 'tp', axis=1, tiled=True)]
    mul x31, local copies, waits for them, and re-layouts: 21.3 us -> 0.29 us  [combine_states(): later[0][:, None, None] * earlier[1] + later[1]]
where the time goes in v1:
time: 719 us; the launch traced here: 717 us
  waiting for transfers between devices  516 us (72%)
  blocking collectives  62.9 us (9%)
  other arithmetic  49.1 us (7%)
  matrix products  28.3 us (4%)
  starting transfers between devices  21.8 us (3%)
  local copies, waits for them, and re-layouts  21 us (3%)
  between operations  17.8 us (2%)
    reduce_scatter x1, waiting for transfers between devices, on_device(): lax.psum_scatter(mix_terms, 'tp', scatter_dimension=1, tiled=True)  88.4 us
    all_gather x1, waiting for transfers between devices, on_device(): lax.all_gather(adapter_down, 'tp', axis=0, tiled=True)  87.6 us
    reduce_scatter x1, waiting for transfers between devices, on_device(): lax.psum_scatter(attn_terms.astype(jnp.bfloat16), 'tp', scatter_dimension...  81.5 us
    ppermute x9, waiting for transfers between devices, from_behind(): return lax.ppermute(block, axis, route)  70.4 us
    all_gather x1, waiting for transfers between devices, on_device(): lax.all_gather(w_bc, 'tp', axis=0, tiled=True)  58.4 us
    all_gather x1, waiting for transfers between devices, on_device(): lax.all_gather(hidden_in, 'tp', axis=1, tiled=True)  56.6 us
    all_gather x1, waiting for transfers between devices, on_device(): lax.all_gather(embeds, 'tp', axis=1, tiled=True)  45.2 us
    all_gather x1, blocking collectives, carried_in_2(): pieces = jax.tree.map(lambda part: lax.all_gather(part, axis), value)  32.8 us
  transfers between devices with their start and end apart: 17, of which 17 were waited for; matrix products, arithmetic and copies ran while one was open for 5% of the time, Pallas kernels for 0%

profile of v1, /device:TPU:8, one launch (start us, length us, event | category | flops | bytes accessed | tf_op | source)
XLA Modules:
  0.0 717.5 jit_solution(101189813368376278)
XLA Ops:
  18.2 56.6 %all-gather.8.cloned.1.call-done = bf16[256,2048]{1,0:T(8,128)(2,1)} async-done(((bf16[256,256]{1,0:T(8,128)(2,1)}), bf16[256,2048]{1,0:T(8,128)(2,1)}) %all-gather.8.cloned.1.call-update) | async-done | bytes 1048592 | tf_op jit(solution)/shard_map/all_gather | solution.py:132
  76.5 58.4 %all-gather.10.cloned.1.call-done = bf16[2048,256]{1,0:T(8,128)(2,1)} async-done(((bf16[256,256]{1,0:T(8,128)(2,1)}), bf16[2048,256]{1,0:T(8,128)(2,1)}) %all-gather.10.cloned.1.call-update) | async-done | bytes 1048592 | tf_op jit(solution)/shard_map/all_gather | solution.py:139
  134.8 2.2 fusion.161
  139.1 1.9 collective-permute-start
  143.5 6.0 collective-permute-done
  152.0 2.0 and_and_fusion.6
  154.1 32.8 %all-gather.1 = f32[32,1,4]{2,1,0:T(1,128)S(1)} all-gather(f32[1,1,4]{2,1,0:T(1,128)S(1)} %bitcast.394), channel_id=1, replica_groups=mesh['req'=32,'tp'=8] {'req'}, dimensions={0}, use_global_device_ids=true | all-gather | bytes 528 | tf_op jit(solution)/shard_map/all_gather | solution.py:20
  189.1 20.2 %all-gather.16.cloned.1.call-done = f32[128,64,128]{2,1,0:T(8,128)} async-done(((f32[4,64,128]{2,1,0:T(8,128)}), f32[128,64,128]{2,1,0:T(8,128)}) %all-gather.16.cloned.1.call-update) | async-done | bytes 4194320 | tf_op jit(solution)/shard_map/all_gather | solution.py:20
  209.4 32.0 %while.9 = (s32[]{:T(128)}, f32[4,64,128]{2,1,0:T(8,128)S(1)}, s32[]{:T(128)}, f32[32,4]{1,0:T(8,128)S(1)}, f32[32,4,64,128]{3,2,1,0:T(8,128)}, /*index=5*/s32[]{:T(128)}, s32[]{:T(128)}) while((s32[]{:T(128)}, f32[4,64,128]{2,1,0:T(8,128)S(1)}, s32[]{:T(128)}, f32[32,4]{1,0:T(8,128)S(1)}, f32[32,4,64,128]{3,2,1,0:T(8,128)}, ...), condition=%wide.region_4.5_spmd.clone, body=%wide.region_3.4_spmd.clone.sunk | while | flops 131076 | bytes 393369 | solution.py:29
  241.8 1.9 multiply_reduce_fusion
  243.7 30.1 %psum.7 = f32[256]{0:T(256)S(1)} all-reduce(f32[256]{0:T(256)S(1)} %get-tuple-element.287), channel_id=1, replica_groups=mesh['req'=32,'tp'=8] {'tp'}, use_global_device_ids=true, to_apply=%region_6.7 | all-reduce | flops 256 | bytes 2048 | tf_op jit(solution)/shard_map/psum | solution.py:211
  277.2 88.4 %reduce-scatter.3.cloned.1.call-done = f32[256,256]{1,0:T(8,128)} async-done(((f32[256,2048]{1,0:T(8,128)}), f32[256,256]{1,0:T(8,128)}) %reduce-scatter.3.cloned.1.call-update) | async-done | bytes 262160 | tf_op jit(solution)/shard_map/reduce_scatter | solution.py:215
  367.6 3.7 all-to-all-start
  371.5 8.8 %copy.136 = bf16[4096,3,256]{0,2,1:T(8,128)(2,1)} copy(bf16[4096,3,256]{2,0,1:T(8,128)(2,1)} %param.38) | data formatting | bytes 12582912 | tf_op args[16]
  383.5 5.2 all-to-all-done
  389.3 45.2 %all-gather.12.cloned.1.call-done = bf16[256,2048]{0,1:T(8,128)(2,1)} async-done(((bf16[256,256]{0,1:T(8,128)(2,1)}), bf16[256,2048]{0,1:T(8,128)(2,1)}) %all-gather.12.cloned.1.call-update) | async-done | bytes 1048592 | tf_op jit(solution)/shard_map/all_gather | solution.py:133
  436.4 87.6 %all-gather.14.cloned.1.call-done = bf16[4096,384]{1,0:T(8,128)(2,1)} async-done(((bf16[512,384]{1,0:T(8,128)(2,1)}), bf16[4096,384]{1,0:T(8,128)(2,1)}) %all-gather.14.cloned.1.call-update) | async-done | bytes 3145744 | tf_op jit(solution)/shard_map/all_gather | solution.py:222
  524.0 5.1 convolution_convert_fusion.1
  530.9 4.8 fusion.1
  537.0 2.1 collective-permute-start.1
  539.8 7.7 %collective-permute-done.1 = bf16[256,2,256]{0,2,1:T(8,128)(2,1)S(1)} collective-permute-done((bf16[256,2,256]{0,2,1:T(8,128)(2,1)S(1)}, bf16[256,2,256]{0,2,1:T(8,128)(2,1)S(1)}, u32[]{:S(2)}, u32[]{:S(2)}) %collective-permute-start.1) | collective-permute-done | bytes 262176 | tf_op jit(solution)/shard_map/ppermute | solution.py:15
  547.5 1.9 collective-permute-start.2
  549.7 8.1 %collective-permute-done.2 = bf16[256,2,256]{0,2,1:T(8,128)(2,1)S(1)} collective-permute-done((bf16[256,2,256]{0,2,1:T(8,128)(2,1)S(1)}, bf16[256,2,256]{0,2,1:T(8,128)(2,1)S(1)}, u32[]{:S(2)}, u32[]{:S(2)}) %collective-permute-start.2) | collective-permute-done | bytes 262176 | tf_op jit(solution)/shard_map/ppermute | solution.py:15
  560.1 8.1 %collective-permute-done.3 = bf16[256,2,256]{0,2,1:T(8,128)(2,1)S(1)} collective-permute-done((bf16[256,2,256]{0,2,1:T(8,128)(2,1)S(1)}, bf16[256,2,256]{0,2,1:T(8,128)(2,1)S(1)}, u32[]{:S(2)}, u32[]{:S(2)}) %collective-permute-start.3) | collective-permute-done | bytes 262176 | tf_op jit(solution)/shard_map/ppermute | solution.py:15
  570.5 8.1 %collective-permute-done.4 = bf16[256,2,256]{0,2,1:T(8,128)(2,1)S(1)} collective-permute-done((bf16[256,2,256]{0,2,1:T(8,128)(2,1)S(1)}, bf16[256,2,256]{0,2,1:T(8,128)(2,1)S(1)}, u32[]{:S(2)}, u32[]{:S(2)}) %collective-permute-start.4) | collective-permute-done | bytes 262176 | tf_op jit(solution)/shard_map/ppermute | solution.py:15
  578.6 2.1 collective-permute-start.5
  581.0 8.1 %collective-permute-done.5 = bf16[256,2,256]{0,2,1:T(8,128)(2,1)S(1)} collective-permute-done((bf16[256,2,256]{0,2,1:T(8,128)(2,1)S(1)}, bf16[256,2,256]{0,2,1:T(8,128)(2,1)S(1)}, u32[]{:S(2)}, u32[]{:S(2)}) %collective-permute-start.5) | collective-permute-done | bytes 262176 | tf_op jit(solution)/shard_map/ppermute | solution.py:15
  591.4 8.1 %collective-permute-done.6 = bf16[256,2,256]{0,2,1:T(8,128)(2,1)S(1)} collective-permute-done((bf16[256,2,256]{0,2,1:T(8,128)(2,1)S(1)}, bf16[256,2,256]{0,2,1:T(8,128)(2,1)S(1)}, u32[]{:S(2)}, u32[]{:S(2)}) %collective-permute-start.6) | collective-permute-done | bytes 262176 | tf_op jit(solution)/shard_map/ppermute | solution.py:15
  601.8 8.1 %collective-permute-done.7 = bf16[256,2,256]{0,2,1:T(8,128)(2,1)S(1)} collective-permute-done((bf16[256,2,256]{0,2,1:T(8,128)(2,1)S(1)}, bf16[256,2,256]{0,2,1:T(8,128)(2,1)S(1)}, u32[]{:S(2)}, u32[]{:S(2)}) %collective-permute-start.7) | collective-permute-done | bytes 262176 | tf_op jit(solution)/shard_map/ppermute | solution.py:15
  609.9 2.1 collective-permute-start.8
  612.4 7.9 %collective-permute-done.8 = bf16[256,2,256]{0,2,1:T(8,128)(2,1)S(1)} collective-permute-done((bf16[256,2,256]{0,2,1:T(8,128)(2,1)S(1)}, bf16[256,2,256]{0,2,1:T(8,128)(2,1)S(1)}, u32[]{:S(2)}, u32[]{:S(2)}) %collective-permute-start.8) | collective-permute-done | bytes 262176 | tf_op jit(solution)/shard_map/ppermute | solution.py:15
  627.5 81.5 %reduce-scatter.5.cloned.1.call-done = bf16[256,256]{1,0:T(8,128)(2,1)} async-done(((bf16[256,2048]{1,0:T(8,128)(2,1)}), bf16[256,256]{1,0:T(8,128)(2,1)}) %reduce-scatter.5.cloned.1.call-update) | async-done | bytes 131088 | tf_op jit(solution)/shard_map/reduce_scatter | solution.py:292
  (261 shorter events, 83.8 us)
Async XLA Ops:
  7.2 266.6 %copy-start = (bf16[256,2048]{1,0:T(8,128)(2,1)S(1)}, bf16[256,2048]{1,0:T(8,128)(2,1)}, u32[]{:S(2)}) copy-start(bf16[256,2048]{1,0:T(8,128)(2,1)} %param.36) | copy-start | bytes 3145732
  7.2 67.7 %all-gather.8.cloned.1.call-start = ((), (), s32[]{:S(2)}) async-start(), calls=%async_computation.3 | async-start | bytes 1179648 | tf_op jit(solution)/shard_map/all_gather | solution.py:132
  7.9 129.1 %copy-start.23 = (f32[2048]{0:T(1024)S(1)}, f32[2048]{0:T(1024)}, u32[]{:S(2)}) copy-start(f32[2048]{0:T(1024)} %param.25) | copy-start | bytes 24580
  7.9 126.9 %all-gather.10.cloned.1.call-start = ((), (), s32[]{:S(2)}) async-start(), calls=%async_computation.4 | async-start | bytes 1179648 | tf_op jit(solution)/shard_map/all_gather | solution.py:139
  8.7 200.7 %all-gather.16.cloned.1.call-start = ((), (), s32[]{:S(2)}) async-start(), calls=%async_computation.9 | async-start | bytes 4325376 | tf_op jit(solution)/shard_map/all_gather | solution.py:20
  74.9 62.2 %copy-start.3 = (bf16[256,2048]{1,0:T(8,128)(2,1)S(1)}, bf16[256,2048]{1,0:T(8,128)(2,1)}, u32[]{:S(2)}) copy-start(bf16[256,2048]{1,0:T(8,128)(2,1)} %all-gather.8.cloned.1.call-done) | copy-start | bytes 3145732
  139.1 10.4 %collective-permute-start = (f32[3,512]{0,1:T(8,128)S(1)}, f32[3,512]{0,1:T(8,128)S(1)}, u32[]{:S(2)}, u32[]{:S(2)}) collective-permute-start(f32[3,512]{0,1:T(8,128)S(1)} %fusion.80), channel_id=1, source_target_pairs={{0,8},{8,16},{16,24},{24,32},{32,40},{40,48},{48,56},{56,64},{64,7... | collective-permute-start | bytes 18440 | tf_op jit(solution)/shard_map/ppermute | solution.py:15
  150.4 38.3 %copy-start.21 = (f32[4]{0:T(128)S(1)}, f32[4]{0:T(128)}, u32[]{:S(2)}) copy-start(f32[4]{0:T(128)} %param.34) | copy-start | bytes 52
  151.6 214.0 %reduce-scatter.3.cloned.1.call-start = ((), (), s32[]{:S(2)}) async-start(), calls=%async_computation.5 | async-start | bytes 2359296 | tf_op jit(solution)/shard_map/reduce_scatter | solution.py:215
  241.8 32.0 %copy-start.20 = (f32[256]{0:T(256)S(1)}, f32[256]{0:T(256)}, u32[]{:S(2)}) copy-start(f32[256]{0:T(256)} %param.35) | copy-start | bytes 3076
  275.7 89.8 %copy-start.16 = (bf16[256,256]{1,0:T(8,128)(2,1)S(1)}, bf16[256,256]{1,0:T(8,128)(2,1)}, u32[]{:S(2)}) copy-start(bf16[256,256]{1,0:T(8,128)(2,1)} %param.22) | copy-start | bytes 393220
  275.7 158.8 %all-gather.12.cloned.1.call-start = ((), (), s32[]{:S(2)}) async-start(), calls=%async_computation.6 | async-start | bytes 1179648 | tf_op jit(solution)/shard_map/all_gather | solution.py:133
  276.6 247.5 %all-gather.14.cloned.1.call-start = ((), (), s32[]{:S(2)}) async-start(), calls=%async_computation.7 | async-start | bytes 3538944 | tf_op jit(solution)/shard_map/all_gather | solution.py:222
  367.6 21.2 %all-to-all-start = ((bf16[8,256,256]{2,1,0:T(8,128)(2,1)}), bf16[8,256,256]{2,1,0:T(8,128)(2,1)S(1)}, u32[]{:S(2)}, u32[]{:S(2)}) async-start(bf16[8,256,256]{2,1,0:T(8,128)(2,1)} %stack.4), calls=%async_computation.1 | async-start | bytes 2097152 | tf_op jit(solution)/shard_map/all_to_all | solution.py:218
  371.2 337.8 %reduce-scatter.5.cloned.1.call-start = ((), (), s32[]{:S(2)}) async-start(), calls=%async_computation.8 | async-start | bytes 1179648 | tf_op jit(solution)/shard_map/reduce_scatter | solution.py:292
  434.5 89.5 %copy-start.7 = (bf16[256,2048]{0,1:T(8,128)(2,1)S(1)}, bf16[256,2048]{0,1:T(8,128)(2,1)}, u32[]{:S(2)}) copy-start(bf16[256,2048]{0,1:T(8,128)(2,1)} %all-gather.12.cloned.1.call-done) | copy-start | bytes 3145732
  537.0 12.5 %copy-start.6 = (pred[256,256]{0,1:T(8,128)(4,1)S(1)}, pred[256,256]{0,1:T(8,128)(4,1)}, u32[]{:S(2)}) copy-start(pred[256,256]{0,1:T(8,128)(4,1)} %get-tuple-element.274) | copy-start | bytes 196612
  537.0 10.5 %collective-permute-start.1 = (bf16[256,2,256]{0,2,1:T(8,128)(2,1)S(1)}, bf16[256,2,256]{0,2,1:T(8,128)(2,1)S(1)}, u32[]{:S(2)}, u32[]{:S(2)}) collective-permute-start(bf16[256,2,256]{0,2,1:T(8,128)(2,1)S(1)} %pad_maximum_fusion.2), channel_id=1, source_target_pairs={{0,8},{8,16},{16,24},{24,32},{32,40},{40,48},{48,56},{56,64},{64,7... | collective-permute-start | bytes 786440 | tf_op jit(solution)/shard_map/ppermute | solution.py:15
  539.3 20.5 %copy-start.12 = (pred[256,256]{0,1:T(8,128)(4,1)S(1)}, pred[256,256]{0,1:T(8,128)(4,1)}, u32[]{:S(2)}) copy-start(pred[256,256]{0,1:T(8,128)(4,1)} %get-tuple-element.266) | copy-start | bytes 196612
  539.5 30.7 %copy-start.11 = (pred[256,256]{0,1:T(8,128)(4,1)S(1)}, pred[256,256]{0,1:T(8,128)(4,1)}, u32[]{:S(2)}) copy-start(pred[256,256]{0,1:T(8,128)(4,1)} %get-tuple-element.267) | copy-start | bytes 196612
  547.5 10.4 %collective-permute-start.2 = (bf16[256,2,256]{0,2,1:T(8,128)(2,1)S(1)}, bf16[256,2,256]{0,2,1:T(8,128)(2,1)S(1)}, u32[]{:S(2)}, u32[]{:S(2)}) collective-permute-start(bf16[256,2,256]{0,2,1:T(8,128)(2,1)S(1)} %collective-permute-done.1), channel_id=1, source_target_pairs={{0,8},{8,16},{16,24},{24,32},{32,40},{40,48},{48,56},{56,64},{64,7... | collective-permute-start | bytes 786440 | tf_op jit(solution)/shard_map/ppermute | solution.py:15
  549.4 31.3 %copy-start.10 = (pred[256,256]{0,1:T(8,128)(4,1)S(1)}, pred[256,256]{0,1:T(8,128)(4,1)}, u32[]{:S(2)}) copy-start(pred[256,256]{0,1:T(8,128)(4,1)} %get-tuple-element.268) | copy-start | bytes 196612
  557.9 10.4 %collective-permute-start.3 = (bf16[256,2,256]{0,2,1:T(8,128)(2,1)S(1)}, bf16[256,2,256]{0,2,1:T(8,128)(2,1)S(1)}, u32[]{:S(2)}, u32[]{:S(2)}) collective-permute-start(bf16[256,2,256]{0,2,1:T(8,128)(2,1)S(1)} %collective-permute-done.2), channel_id=1, source_target_pairs={{0,8},{8,16},{16,24},{24,32},{32,40},{40,48},{48,56},{56,64},{64,7... | collective-permute-start | bytes 786440 | tf_op jit(solution)/shard_map/ppermute | solution.py:15
  559.8 31.3 %copy-start.9 = (pred[256,256]{0,1:T(8,128)(4,1)S(1)}, pred[256,256]{0,1:T(8,128)(4,1)}, u32[]{:S(2)}) copy-start(pred[256,256]{0,1:T(8,128)(4,1)} %get-tuple-element.269) | copy-start | bytes 196612
  568.2 10.4 %collective-permute-start.4 = (bf16[256,2,256]{0,2,1:T(8,128)(2,1)S(1)}, bf16[256,2,256]{0,2,1:T(8,128)(2,1)S(1)}, u32[]{:S(2)}, u32[]{:S(2)}) collective-permute-start(bf16[256,2,256]{0,2,1:T(8,128)(2,1)S(1)} %collective-permute-done.3), channel_id=1, source_target_pairs={{0,8},{8,16},{16,24},{24,32},{32,40},{40,48},{48,56},{56,64},{64,7... | collective-permute-start | bytes 786440 | tf_op jit(solution)/shard_map/ppermute | solution.py:15
  570.2 31.3 %copy-start.8 = (pred[256,256]{0,1:T(8,128)(4,1)S(1)}, pred[256,256]{0,1:T(8,128)(4,1)}, u32[]{:S(2)}) copy-start(pred[256,256]{0,1:T(8,128)(4,1)} %get-tuple-element.270) | copy-start | bytes 196612
  578.6 33.5 %copy-start.5 = (pred[256,256]{0,1:T(8,128)(4,1)S(1)}, pred[256,256]{0,1:T(8,128)(4,1)}, u32[]{:S(2)}) copy-start(pred[256,256]{0,1:T(8,128)(4,1)} %get-tuple-element.272) | copy-start | bytes 196612
  578.6 10.5 %collective-permute-start.5 = (bf16[256,2,256]{0,2,1:T(8,128)(2,1)S(1)}, bf16[256,2,256]{0,2,1:T(8,128)(2,1)S(1)}, u32[]{:S(2)}, u32[]{:S(2)}) collective-permute-start(bf16[256,2,256]{0,2,1:T(8,128)(2,1)S(1)} %collective-permute-done.4), channel_id=1, source_target_pairs={{0,8},{8,16},{16,24},{24,32},{32,40},{40,48},{48,56},{56,64},{64,7... | collective-permute-start | bytes 786440 | tf_op jit(solution)/shard_map/ppermute | solution.py:15
  589.2 10.4 %collective-permute-start.6 = (bf16[256,2,256]{0,2,1:T(8,128)(2,1)S(1)}, bf16[256,2,256]{0,2,1:T(8,128)(2,1)S(1)}, u32[]{:S(2)}, u32[]{:S(2)}) collective-permute-start(bf16[256,2,256]{0,2,1:T(8,128)(2,1)S(1)} %collective-permute-done.5), channel_id=1, source_target_pairs={{0,8},{8,16},{16,24},{24,32},{32,40},{40,48},{48,56},{56,64},{64,7... | collective-permute-start | bytes 786440 | tf_op jit(solution)/shard_map/ppermute | solution.py:15
  591.1 29.2 %copy-start.15 = (pred[256,256]{0,1:T(8,128)(4,1)S(1)}, pred[256,256]{0,1:T(8,128)(4,1)}, u32[]{:S(2)}) copy-start(pred[256,256]{0,1:T(8,128)(4,1)} %get-tuple-element.273) | copy-start | bytes 196612
  599.5 10.4 %collective-permute-start.7 = (bf16[256,2,256]{0,2,1:T(8,128)(2,1)S(1)}, bf16[256,2,256]{0,2,1:T(8,128)(2,1)S(1)}, u32[]{:S(2)}, u32[]{:S(2)}) collective-permute-start(bf16[256,2,256]{0,2,1:T(8,128)(2,1)S(1)} %collective-permute-done.6), channel_id=1, source_target_pairs={{0,8},{8,16},{16,24},{24,32},{32,40},{40,48},{48,56},{56,64},{64,7... | collective-permute-start | bytes 786440 | tf_op jit(solution)/shard_map/ppermute | solution.py:15
  609.9 10.4 %collective-permute-start.8 = (bf16[256,2,256]{0,2,1:T(8,128)(2,1)S(1)}, bf16[256,2,256]{0,2,1:T(8,128)(2,1)S(1)}, u32[]{:S(2)}, u32[]{:S(2)}) collective-permute-start(bf16[256,2,256]{0,2,1:T(8,128)(2,1)S(1)} %collective-permute-done.7), channel_id=1, source_target_pairs={{0,8},{8,16},{16,24},{24,32},{32,40},{40,48},{48,56},{56,64},{64,7... | collective-permute-start | bytes 786440 | tf_op jit(solution)/shard_map/ppermute | solution.py:15
  (11 other events, 32.7 us)
Sparse Core Ops, SparseCore 0:
  10.5 64.3 all-gather.7
  77.5 57.2 all-gather.9
  151.7 57.6 all-gather.15
  275.9 89.6 reduce-scatter.2
  368.6 65.8 all-gather.11
  437.0 87.0 all-gather.13
  626.0 82.9 reduce-scatter.4
